TPU v7x, 128 devices: a whole 4x4x4 slice. The times are simulated.
128 devices in a mesh: site: 4 (over y_lo, core), section: 4 (over x), tensor: 8 (over y_hi, z).
Axes of the slice: x: 4, y: 4 (y_hi: 2, y_lo: 2; y = y_hi * 2 + y_lo), z: 4, core: 2. Of those that a mesh axis runs over, the one named last changes fastest.
Arguments:
- inputs: bfloat16 [4, 4, 256, 896], P('site'), may hold values from -6 to 6
- out_grad: bfloat16 [4, 4, 256, 896], P('site'), may hold values from -0.1875 to 0.1875
- local_gate: bfloat16 [4, 4, 896, 4864], P('site', 'section', None, 'tensor'), may hold values from -0.1875 to 0.1875
- local_up: bfloat16 [4, 4, 896, 4864], P('site', 'section', None, 'tensor'), may hold values from -0.1875 to 0.1875
- local_down: bfloat16 [4, 4, 4864, 896], P('site', 'section', 'tensor'), may hold values from -0.078125 to 0.078125
- local_gain: float32 [4, 4, 896], P('site', 'section'), may hold values from 0.5 to 1.5
- anchor_gate: bfloat16 [4, 896, 4864], P('section', None, 'tensor'), may hold values from -0.1875 to 0.1875
- anchor_up: bfloat16 [4, 896, 4864], P('section', None, 'tensor'), may hold values from -0.1875 to 0.1875
- anchor_down: bfloat16 [4, 4864, 896], P('section', 'tensor'), may hold values from -0.078125 to 0.078125
- anchor_gain: float32 [4, 896], P('section'), may hold values from 0.5 to 1.5
Outputs:
- round_gate: float32 [4, 896, 4864], P('section', None, 'tensor')
- round_up: float32 [4, 896, 4864], P('section', None, 'tensor')
- round_down: float32 [4, 4864, 896], P('section', 'tensor')
- round_gain: float32 [4, 896], P('section')
All inputs are finite; a program needn't handle non-finite values.
Results may differ from a plain program's by a relative error of at most 0.03.
Values may be sent and summed in bfloat16 or wider, within the bound.
No kernel may reach another device: no remote copies, remote signals or barrier semaphores. Data moves between devices by JAX's collectives and lax.ppermute only.
A program may use at most 128 MiB of HBM per device.

v0:
```python
import jax
import jax.numpy as jnp
from jax import lax
from jax.sharding import PartitionSpec as P

epsilon = 1e-06
prox_weight = 1.0


def passed_along(block, axis, distance):
    devices = range(lax.axis_size(axis))
    route = [(i - distance, i) for i in devices if i - distance in devices]
    return lax.ppermute(block, axis, route)


def norm_rows(wide_rows, gain_row):
    row_scale = lax.rsqrt(jnp.mean(wide_rows * wide_rows, axis=-1, keepdims=True) + epsilon)
    unit_rows = wide_rows * row_scale
    return (unit_rows, row_scale, (unit_rows * gain_row).astype(jnp.bfloat16))


def contract_rows(left_side, right_side):
    return lax.dot_general(
        left_side, right_side, (((0,), (0,)), ((), ())), preferred_element_type=jnp.float32
    )


def contract_cols(left_side, right_side):
    return lax.dot_general(
        left_side, right_side, (((1,), (1,)), ((), ())), preferred_element_type=jnp.float32
    )


def pick_block(blocks, block_index):
    return lax.dynamic_index_in_dim(blocks, block_index, 0, keepdims=False)


def shards(
    inputs,
    out_grad,
    local_gate,
    local_up,
    local_down,
    local_gain,
    anchor_gate,
    anchor_up,
    anchor_down,
    anchor_gain,
):
    w_gate = local_gate[0, 0]
    w_up = local_up[0, 0]
    w_down = local_down[0, 0]
    gain_row = local_gain[0, 0]
    site_feed = inputs[0]
    loss_grad = out_grad[0]
    micro_count = site_feed.shape[0]
    row_count = site_feed.shape[1]
    feature_count = site_feed.shape[2]
    section_count = lax.axis_size("section")
    section_index = lax.axis_index("section")
    site_count = lax.axis_size("site")
    tick_count = micro_count + section_count - 1

    def hidden_of(normed):
        gate_pre = jnp.dot(normed, w_gate, preferred_element_type=jnp.float32)
        up_pre = jnp.dot(normed, w_up, preferred_element_type=jnp.float32)
        return (gate_pre, up_pre, jax.nn.sigmoid(gate_pre))

    def slot_of(micro_index):
        is_valid = (micro_index >= 0) & (micro_index < micro_count)
        return (is_valid, jnp.clip(micro_index, 0, micro_count - 1))

    weight_grads = (
        jnp.zeros(w_gate.shape, jnp.float32),
        jnp.zeros(w_up.shape, jnp.float32),
        jnp.zeros(w_down.shape, jnp.float32),
    )
    gain_grad = jnp.zeros((feature_count,), jnp.float32)
    stored = jnp.zeros((micro_count, row_count, feature_count), jnp.bfloat16)
    received = jnp.zeros((row_count, feature_count), jnp.bfloat16)
    for moment in range(tick_count):
        if moment < micro_count:
            inject = site_feed[moment]
        else:
            inject = jnp.zeros_like(received)
        current = jnp.where(section_index == 0, inject, received)
        is_valid, mb_slot = slot_of(moment - section_index)
        previous = pick_block(stored, mb_slot)
        stored = lax.dynamic_update_index_in_dim(
            stored, jnp.where(is_valid, current, previous), mb_slot, 0
        )
        if moment + 1 < tick_count:
            wide_in = current.astype(jnp.float32)
            unit_rows, row_scale, normed = norm_rows(wide_in, gain_row)
            make_gate_pre, make_up_pre, make_sig_gate = hidden_of(normed)
            partial_value = jnp.dot(
                (make_gate_pre * make_sig_gate * make_up_pre).astype(jnp.bfloat16),
                w_down,
                preferred_element_type=jnp.float32,
            )
            summed = lax.psum(partial_value.astype(jnp.bfloat16), "tensor").astype(jnp.float32)
            received = passed_along((wide_in + summed).astype(jnp.bfloat16), "section", 1)
    received = jnp.zeros((row_count, feature_count), jnp.bfloat16)
    for moment in range(tick_count):
        is_valid, mb_slot = slot_of(moment - (section_count - 1 - section_index))
        incoming = jnp.where(
            section_index == section_count - 1, pick_block(loss_grad, mb_slot), received
        )
        incoming = jnp.where(is_valid, incoming, jnp.zeros_like(incoming))
        wide_in = pick_block(stored, mb_slot).astype(jnp.float32)
        unit_rows, row_scale, normed = norm_rows(wide_in, gain_row)
        local_weight_grads = weight_grads
        local_gate_pre, local_up_pre, sig_gate = hidden_of(normed)
        silu_gate = local_gate_pre * sig_gate
        hidden = (silu_gate * local_up_pre).astype(jnp.bfloat16)
        d_hidden = contract_cols(incoming, w_down)
        d_gate_pre = (
            d_hidden * local_up_pre * sig_gate * (1.0 + local_gate_pre * (1.0 - sig_gate))
        ).astype(jnp.bfloat16)
        d_up_pre = (d_hidden * silu_gate).astype(jnp.bfloat16)
        local_weight_grads = (
            local_weight_grads[0] + contract_rows(normed, d_gate_pre),
            local_weight_grads[1] + contract_rows(normed, d_up_pre),
            local_weight_grads[2] + contract_rows(hidden, incoming),
        )
        weight_grads, d_gate_pre, d_up_pre = (local_weight_grads, d_gate_pre, d_up_pre)
        d_part = contract_cols(d_gate_pre, w_gate) + contract_cols(d_up_pre, w_up)
        d_norm = lax.psum(d_part.astype(jnp.bfloat16), "tensor").astype(jnp.float32)
        gain_grad = gain_grad + jnp.sum(d_norm * unit_rows, axis=0)
        d_unit = d_norm * gain_row
        sent_back = (
            incoming.astype(jnp.float32)
            + row_scale
            * (d_unit - unit_rows * jnp.mean(d_unit * unit_rows, axis=-1, keepdims=True))
        ).astype(jnp.bfloat16)
        if moment + 1 < tick_count:
            received = passed_along(sent_back, "section", -1)
    gain_term = gain_grad + prox_weight * (gain_row - anchor_gain[0])
    gate_term = weight_grads[0] + prox_weight * (
        w_gate.astype(jnp.float32) - anchor_gate[0].astype(jnp.float32)
    )
    up_term = weight_grads[1] + prox_weight * (
        w_up.astype(jnp.float32) - anchor_up[0].astype(jnp.float32)
    )
    down_term = weight_grads[2] + prox_weight * (
        w_down.astype(jnp.float32) - anchor_down[0].astype(jnp.float32)
    )
    gate_total, up_total, down_total, gain_total = (
        lax.psum(gate_term.astype(jnp.bfloat16), "site").astype(jnp.float32),
        lax.psum(up_term.astype(jnp.bfloat16), "site").astype(jnp.float32),
        lax.psum(down_term.astype(jnp.bfloat16), "site").astype(jnp.float32),
        lax.psum(gain_term.astype(jnp.bfloat16), "site").astype(jnp.float32),
    )
    return (
        (gate_total / site_count)[None],
        (up_total / site_count)[None],
        (down_total / site_count)[None],
        (gain_total / site_count)[None],
    )


def solution(mesh):
    in_specs = (
        P("site", None, None, None),
        P("site", None, None, None),
        P("site", "section", None, "tensor"),
        P("site", "section", None, "tensor"),
        P("site", "section", "tensor", None),
        P("site", "section", None),
        P("section", None, "tensor"),
        P("section", None, "tensor"),
        P("section", "tensor", None),
        P("section", None),
    )
    out_specs = (
        P("section", None, "tensor"),
        P("section", None, "tensor"),
        P("section", "tensor", None),
        P("section", None),
    )
    return jax.shard_map(shards, mesh=mesh, in_specs=in_specs, out_specs=out_specs, check_vma=False)
```

profile of v0, /device:TPU:28, one launch (start us, length us, event | category | flops | bytes accessed | tf_op | source)
XLA Modules:
  0.0 1423.5 jit_solution(9092616407235688627)
XLA Ops:
  9.3 2.0 fusion.158
  11.3 3.5 convolution_convert_fusion.5
  14.9 86.4 %all-reduce.16.cloned.1.call-done = bf16[256,896]{1,0:T(8,128)(2,1)} async-done(((bf16[256,896]{1,0:T(8,128)(2,1)}), bf16[256,896]{1,0:T(8,128)(2,1)}) %all-reduce.16.cloned.1.call-update) | async-done | bytes 458768 | tf_op jit(solution)/shard_map/psum | solution.py:101
  102.6 3.1 collective-permute-start
  105.7 7.3 collective-permute-done
  115.7 3.9 convolution_convert_fusion.4
  119.6 83.8 %all-reduce.18.cloned.1.call-done = bf16[256,896]{1,0:T(8,128)(2,1)} async-done(((bf16[256,896]{1,0:T(8,128)(2,1)}), bf16[256,896]{1,0:T(8,128)(2,1)}) %all-reduce.18.cloned.1.call-update) | async-done | bytes 458768 | tf_op jit(solution)/shard_map/psum | solution.py:101
  204.6 3.1 collective-permute-start.1
  207.7 7.3 collective-permute-done.1
  217.6 3.9 convolution_convert_fusion.3
  221.6 83.8 %all-reduce.20.cloned.1.call-done = bf16[256,896]{1,0:T(8,128)(2,1)} async-done(((bf16[256,896]{1,0:T(8,128)(2,1)}), bf16[256,896]{1,0:T(8,128)(2,1)}) %all-reduce.20.cloned.1.call-update) | async-done | bytes 458768 | tf_op jit(solution)/shard_map/psum | solution.py:101
  306.6 3.1 collective-permute-start.2
  309.7 7.3 collective-permute-done.2
  319.7 3.9 convolution_convert_fusion.2
  323.6 83.8 %all-reduce.22.cloned.1.call-done = bf16[256,896]{1,0:T(8,128)(2,1)} async-done(((bf16[256,896]{1,0:T(8,128)(2,1)}), bf16[256,896]{1,0:T(8,128)(2,1)}) %all-reduce.22.cloned.1.call-update) | async-done | bytes 458768 | tf_op jit(solution)/shard_map/psum | solution.py:101
  409.3 3.1 collective-permute-start.3
  412.4 7.5 collective-permute-done.3
  420.7 3.7 convolution_convert_fusion.1
  426.1 82.2 %all-reduce.24.cloned.1.call-done = bf16[256,896]{1,0:T(8,128)(2,1)} async-done(((bf16[256,896]{1,0:T(8,128)(2,1)}), bf16[256,896]{1,0:T(8,128)(2,1)}) %all-reduce.24.cloned.1.call-update) | async-done | bytes 458768 | tf_op jit(solution)/shard_map/psum | solution.py:101
  509.6 3.3 collective-permute-start.4
  513.9 6.1 collective-permute-done.4
  522.1 4.4 convolution_convert_fusion
  528.1 82.2 %all-reduce.26.cloned.1.call-done = bf16[256,896]{1,0:T(8,128)(2,1)} async-done(((bf16[256,896]{1,0:T(8,128)(2,1)}), bf16[256,896]{1,0:T(8,128)(2,1)}) %all-reduce.26.cloned.1.call-update) | async-done | bytes 458768 | tf_op jit(solution)/shard_map/psum | solution.py:101
  611.7 3.1 collective-permute-start.5
  615.1 7.0 collective-permute-done.5
  626.2 2.0 fusion.367
  629.7 2.0 fusion.365
  631.7 2.9 fusion.294
  634.6 78.8 %all-reduce.28.cloned.1.call-done = bf16[256,896]{1,0:T(8,128)(2,1)} async-done(((bf16[256,896]{1,0:T(8,128)(2,1)}), bf16[256,896]{1,0:T(8,128)(2,1)}) %all-reduce.28.cloned.1.call-update) | async-done | bytes 458768 | tf_op jit(solution)/shard_map/psum | solution.py:128
  716.6 2.5 collective-permute-start.6
  720.3 6.6 collective-permute-done.6
  729.3 2.0 fusion.363
  733.0 3.0 fusion.361
  737.9 78.7 %all-reduce.30.cloned.1.call-done = bf16[256,896]{1,0:T(8,128)(2,1)} async-done(((bf16[256,896]{1,0:T(8,128)(2,1)}), bf16[256,896]{1,0:T(8,128)(2,1)}) %all-reduce.30.cloned.1.call-update) | async-done | bytes 458768 | tf_op jit(solution)/shard_map/psum | solution.py:128
  816.6 2.0 fusion.192
  826.0 2.6 collective-permute-start.7
  830.1 6.4 collective-permute-done.7
  842.5 82.3 %all-reduce.32.cloned.1.call-done = bf16[256,896]{1,0:T(8,128)(2,1)} async-done(((bf16[256,896]{1,0:T(8,128)(2,1)}), bf16[256,896]{1,0:T(8,128)(2,1)}) %all-reduce.32.cloned.1.call-update) | async-done | bytes 458768 | tf_op jit(solution)/shard_map/psum | solution.py:128
  927.8 2.5 collective-permute-start.8
  933.2 5.0 collective-permute-done.8
  942.7 3.0 fusion.359
  947.6 78.8 %all-reduce.34.cloned.1.call-done = bf16[256,896]{1,0:T(8,128)(2,1)} async-done(((bf16[256,896]{1,0:T(8,128)(2,1)}), bf16[256,896]{1,0:T(8,128)(2,1)}) %all-reduce.34.cloned.1.call-update) | async-done | bytes 458768 | tf_op jit(solution)/shard_map/psum | solution.py:128
  1029.4 3.0 collective-permute-start.9
  1032.4 1.9 fusion.357
  1034.4 2.0 fusion.355
  1036.4 3.9 collective-permute-done.9
  1045.7 3.0 fusion.353
  1050.6 78.9 %all-reduce.36.cloned.1.call-done = bf16[256,896]{1,0:T(8,128)(2,1)} async-done(((bf16[256,896]{1,0:T(8,128)(2,1)}), bf16[256,896]{1,0:T(8,128)(2,1)}) %all-reduce.36.cloned.1.call-update) | async-done | bytes 458768 | tf_op jit(solution)/shard_map/psum | solution.py:128
  1132.5 2.6 collective-permute-start.10
  1135.2 2.0 fusion.351
  1139.1 4.0 collective-permute-done.10
  1147.7 3.0 fusion.349
  1152.6 78.9 %all-reduce.38.cloned.1.call-done = bf16[256,896]{1,0:T(8,128)(2,1)} async-done(((bf16[256,896]{1,0:T(8,128)(2,1)}), bf16[256,896]{1,0:T(8,128)(2,1)}) %all-reduce.38.cloned.1.call-update) | async-done | bytes 458768 | tf_op jit(solution)/shard_map/psum | solution.py:128
  1234.4 2.6 collective-permute-start.11
  1237.1 2.0 fusion.345
  1241.0 4.0 collective-permute-done.11
  1249.9 7.6 fusion.3
  1260.6 3.4 fusion.1
  1266.1 2.2 fusion.5
  1269.1 64.3 %all-reduce.40.cloned.1.call-done = bf16[256,896]{1,0:T(8,128)(2,1)} async-done(((bf16[256,896]{1,0:T(8,128)(2,1)}), bf16[256,896]{1,0:T(8,128)(2,1)}) %all-reduce.40.cloned.1.call-update) | async-done | bytes 458768 | tf_op jit(solution)/shard_map/psum | solution.py:128
  1334.6 5.8 psum.135
  1341.0 70.6 %all-reduce.42.cloned.1.call-done = (bf16[896,608]{0,1:T(8,128)(2,1)}, bf16[896,608]{0,1:T(8,128)(2,1)}, bf16[608,896]{1,0:T(8,128)(2,1)}) async-done(((bf16[896,608]{0,1:T(8,128)(2,1)}, bf16[896,608]{0,1:T(8,128)(2,1)}, bf16[608,896]{1,0:T(8,128)(2,1)}), (bf16[896,608]{0,1:T(8,128)(2,1)}, bf16[896,608]{0,1:T(8,128)(2,1)}, bf16[608,896]{1,0:T(8,128)(2,1)})) %all-reduce.42.cloned.1.call-update) | async-done | bytes 3268624 | tf_op jit(solution)/shard_map/psum | solution.py:149
  1411.6 2.9 multiply_bitcast_fusion
  1414.4 2.3 multiply_bitcast_fusion.1
  (324 shorter events, 107.5 us)
Async XLA Ops:
  7.2 94.1 %all-reduce.16.cloned.1.call-start = ((), (), s32[]{:S(2)}) async-start(), calls=%async_computation | async-start | bytes 917504 | tf_op jit(solution)/shard_map/psum | solution.py:101
  14.8 99.4 %copy-start = (bf16[1,1,896,608]{2,3,1,0:T(8,128)(2,1)S(1)}, bf16[1,1,896,608]{2,3,1,0:T(8,128)(2,1)}, u32[]{:S(2)}) copy-start(bf16[1,1,896,608]{2,3,1,0:T(8,128)(2,1)} %param.12) | copy-start | bytes 3268612
  14.9 188.6 %all-reduce.18.cloned.1.call-start = ((), (), s32[]{:S(2)}) async-start(), calls=%async_computation.1 | async-start | bytes 917504 | tf_op jit(solution)/shard_map/psum | solution.py:101
  102.6 10.4 collective-permute-start
  114.2 89.2 %copy-start.22 = (bf16[256,896]{1,0:T(8,128)(2,1)}, bf16[256,896]{1,0:T(8,128)(2,1)S(1)}, u32[]{:S(2)}) copy-start(bf16[256,896]{1,0:T(8,128)(2,1)S(1)} %get-tuple-element.30) | copy-start | bytes 1376260
  119.6 185.9 %all-reduce.20.cloned.1.call-start = ((), (), s32[]{:S(2)}) async-start(), calls=%async_computation.2 | async-start | bytes 917504 | tf_op jit(solution)/shard_map/psum | solution.py:101
  204.6 10.4 collective-permute-start.1
  216.2 89.2 %copy-start.23 = (bf16[256,896]{1,0:T(8,128)(2,1)}, bf16[256,896]{1,0:T(8,128)(2,1)S(1)}, u32[]{:S(2)}) copy-start(bf16[256,896]{1,0:T(8,128)(2,1)S(1)} %get-tuple-element.28) | copy-start | bytes 1376260
  221.6 185.8 %all-reduce.22.cloned.1.call-start = ((), (), s32[]{:S(2)}) async-start(), calls=%async_computation.3 | async-start | bytes 917504 | tf_op jit(solution)/shard_map/psum | solution.py:101
  306.6 10.4 collective-permute-start.2
  318.2 89.2 %copy-start.25 = (bf16[256,896]{1,0:T(8,128)(2,1)}, bf16[256,896]{1,0:T(8,128)(2,1)S(1)}, u32[]{:S(2)}) copy-start(bf16[256,896]{1,0:T(8,128)(2,1)S(1)} %get-tuple-element.26) | copy-start | bytes 1376260
  323.6 184.7 %all-reduce.24.cloned.1.call-start = ((), (), s32[]{:S(2)}) async-start(), calls=%async_computation.4 | async-start | bytes 917504 | tf_op jit(solution)/shard_map/psum | solution.py:101
  409.3 10.6 collective-permute-start.3
  424.5 185.9 %all-reduce.26.cloned.1.call-start = ((), (), s32[]{:S(2)}) async-start(), calls=%async_computation.5 | async-start | bytes 917504 | tf_op jit(solution)/shard_map/psum | solution.py:101
  509.6 10.4 collective-permute-start.4
  526.5 186.8 %all-reduce.28.cloned.1.call-start = ((), (), s32[]{:S(2)}) async-start(), calls=%async_computation.6 | async-start | bytes 917504 | tf_op jit(solution)/shard_map/psum | solution.py:128
  528.1 86.7 %copy-start.21 = (bf16[256,896]{1,0:T(8,128)(2,1)S(1)}, bf16[256,896]{1,0:T(8,128)(2,1)}, u32[]{:S(2)}) copy-start(bf16[256,896]{1,0:T(8,128)(2,1)} %copy-done.20) | copy-start | bytes 1376260
  611.7 10.4 collective-permute-start.5
  614.8 7.6 copy-start.2
  629.6 187.0 %all-reduce.30.cloned.1.call-start = ((), (), s32[]{:S(2)}) async-start(), calls=%async_computation.7 | async-start | bytes 917504 | tf_op jit(solution)/shard_map/psum | solution.py:128
  716.6 10.4 collective-permute-start.6
  719.7 9.0 copy-start.80
  719.7 8.4 copy-start.49
  720.3 8.4 copy-start.82
  732.8 192.0 %all-reduce.32.cloned.1.call-start = ((), (), s32[]{:S(2)}) async-start(), calls=%async_computation.8 | async-start | bytes 917504 | tf_op jit(solution)/shard_map/psum | solution.py:128
  819.2 18.4 %copy-start.76 = (f32[256,608]{0,1:T(8,128)}, f32[256,608]{0,1:T(8,128)S(1)}, u32[]{:S(2)}) copy-start(f32[256,608]{0,1:T(8,128)S(1)} %fusion.100) | copy-start | bytes 1867780
  819.8 17.8 %copy-start.78 = (f32[256,608]{0,1:T(8,128)}, f32[256,608]{0,1:T(8,128)S(1)}, u32[]{:S(2)}) copy-start(f32[256,608]{0,1:T(8,128)S(1)} %fusion.138) | copy-start | bytes 1867780
  826.0 11.6 copy-start.50
  826.0 10.5 collective-permute-start.7
  837.6 88.7 %copy-start.26 = (bf16[256,896]{1,0:T(8,128)(2,1)}, bf16[256,896]{1,0:T(8,128)(2,1)S(1)}, u32[]{:S(2)}) copy-start(bf16[256,896]{1,0:T(8,128)(2,1)S(1)} %fusion.292) | copy-start | bytes 1376260
  841.0 185.4 %all-reduce.34.cloned.1.call-start = ((), (), s32[]{:S(2)}) async-start(), calls=%async_computation.9 | async-start | bytes 917504 | tf_op jit(solution)/shard_map/psum | solution.py:128
  927.8 10.4 collective-permute-start.8
  931.7 7.5 copy-start.51
  931.7 7.5 copy-start.72
  931.7 7.6 copy-start.74
  942.6 186.9 %all-reduce.36.cloned.1.call-start = ((), (), s32[]{:S(2)}) async-start(), calls=%async_computation.10 | async-start | bytes 917504 | tf_op jit(solution)/shard_map/psum | solution.py:128
  1026.4 6.0 copy-start.33
  1029.4 10.9 collective-permute-start.9
  1034.3 7.8 copy-start.52
  1034.4 7.8 copy-start.68
  1034.4 7.8 copy-start.70
  1045.6 185.9 %all-reduce.38.cloned.1.call-start = ((), (), s32[]{:S(2)}) async-start(), calls=%async_computation.11 | async-start | bytes 917504 | tf_op jit(solution)/shard_map/psum | solution.py:128
  1050.6 84.6 %copy-start.43 = (bf16[256,608]{0,1:T(8,128)(2,1)S(1)}, bf16[256,608]{0,1:T(8,128)(2,1)}, u32[]{:S(2)}) copy-start(bf16[256,608]{0,1:T(8,128)(2,1)} %copy-done.42) | copy-start | bytes 933892
  1132.5 10.5 collective-permute-start.10
  1137.1 7.0 copy-start.53
  1137.1 7.0 copy-start.64
  1137.1 7.0 copy-start.66
  1147.6 185.7 %all-reduce.40.cloned.1.call-start = ((), (), s32[]{:S(2)}) async-start(), calls=%async_computation.12 | async-start | bytes 917504 | tf_op jit(solution)/shard_map/psum | solution.py:128
  1234.4 10.5 collective-permute-start.11
  1239.0 5.9 copy-start.54
  1239.0 5.9 copy-start.60
  1239.0 5.9 copy-start.62
  1249.6 162.0 %all-reduce.42.cloned.1.call-start = ((), (), s32[]{:S(2)}) async-start(), calls=%async_computation.13 | async-start | bytes 6537216 | tf_op jit(solution)/shard_map/psum | solution.py:149
  1249.8 7.7 copy-start.15
  1249.8 7.7 copy-start.16
  1249.8 7.7 copy-start.17
  1249.8 8.5 copy-start.18
  1249.8 9.1 copy-start.19
  1249.8 9.7 copy-start.30
  1249.9 9.9 copy-start.55
  1249.9 10.2 copy-start.56
  1249.9 10.4 copy-start.61
  1249.9 10.5 copy-start.63
  1249.9 10.6 copy-start.85
  (53 other events, 152.3 us)
Sparse Core Ops, SparseCore 0:
  15.0 86.2 all-reduce.15
  119.7 83.6 all-reduce.17
  221.7 83.6 all-reduce.19
  323.7 83.6 all-reduce.21
  424.6 83.6 all-reduce.23
  526.6 83.6 all-reduce.25
  629.7 83.6 all-reduce.27
  732.9 83.6 all-reduce.29
  841.1 83.6 all-reduce.31
  942.7 83.6 all-reduce.33
  1045.7 83.6 all-reduce.35
  1147.8 83.6 all-reduce.37
  1249.7 83.6 all-reduce.39
  1336.5 74.9 all-reduce.41
where the time goes:
time: 1440 us; the launch traced here: 1420 us
  waiting for transfers between devices  1190 us (83%)
  matrix products  121 us (8%)
  other arithmetic  47.2 us (3%)
  starting transfers between devices  35.4 us (2%)
  between operations  15.5 us (1%)
    psum x7, waiting for transfers between devices, shards(): d_norm = lax.psum(d_part.astype(jnp.bfloat16), 'tensor').astype(jnp.float32)  541 us
    psum x6, waiting for transfers between devices, shards(): lax.psum(partial_value.astype(jnp.bfloat16), 'tensor').astype(jnp.float32)  502 us
    ppermute x12, waiting for transfers between devices, passed_along(): return lax.ppermute(block, axis, route)  72.3 us
    psum x1, waiting for transfers between devices, shards(): lax.psum(gate_term.astype(jnp.bfloat16), 'site').astype(jnp.float32)  70.6 us
    dot_general x21, matrix products, contract_rows(): lax.dot_general(left_side, right_side, (((0,), (0,)), ((), ())), preferre...  53.5 us
    ppermute x12, starting transfers between devices, passed_along(): return lax.ppermute(block, axis, route)  34.4 us
  transfers between devices with their start and end apart: 26, of which 26 were waited for; matrix products, arithmetic and copies ran while one was open for 4% of the time, Pallas kernels for 0%

commit v1 on v0

v1 whole, which is shorter than its diff:
```python
import jax
import jax.numpy as jnp
from jax import lax
from jax.sharding import PartitionSpec as P

epsilon = 1e-06
prox_weight = 1.0


def passed_along(block, axis, distance):
    devices = range(lax.axis_size(axis))
    route = [(i - distance, i) for i in devices if i - distance in devices]
    return lax.ppermute(block, axis, route)


def norm_rows(wide_rows, gain_row):
    row_scale = lax.rsqrt(jnp.mean(wide_rows * wide_rows, axis=-1, keepdims=True) + epsilon)
    unit_rows = wide_rows * row_scale
    return (unit_rows, row_scale, (unit_rows * gain_row).astype(jnp.bfloat16))


def contract_rows(left_side, right_side):
    return lax.dot_general(
        left_side, right_side, (((0,), (0,)), ((), ())), preferred_element_type=jnp.float32
    )


def contract_cols(left_side, right_side):
    return lax.dot_general(
        left_side, right_side, (((1,), (1,)), ((), ())), preferred_element_type=jnp.float32
    )


def pick_block(blocks, block_index):
    return lax.dynamic_index_in_dim(blocks, block_index, 0, keepdims=False)


def gather_rows(chunks, tensor_count):
    n, c, d = chunks.shape
    spread = jnp.broadcast_to(chunks[:, None], (n, tensor_count, c, d))
    got = lax.all_to_all(spread, "tensor", 1, 1, tiled=False)
    return got.reshape(n, tensor_count * c, d)


def scatter_rows(parts, tensor_count):
    n, r, d = parts.shape
    split = parts.reshape(n, tensor_count, r // tensor_count, d)
    got = lax.all_to_all(split, "tensor", 1, 1, tiled=False)
    return jnp.sum(got.astype(jnp.float32), axis=1)


def shards(
    inputs,
    out_grad,
    local_gate,
    local_up,
    local_down,
    local_gain,
    anchor_gate,
    anchor_up,
    anchor_down,
    anchor_gain,
):
    w_gate = local_gate[0, 0]
    w_up = local_up[0, 0]
    w_down = local_down[0, 0]
    gain_row = local_gain[0, 0]
    site_feed = inputs[0]
    loss_grad = out_grad[0]
    micro_count = site_feed.shape[0]
    row_count = site_feed.shape[1]
    feature_count = site_feed.shape[2]
    section_count = lax.axis_size("section")
    section_index = lax.axis_index("section")
    tensor_count = lax.axis_size("tensor")
    tensor_index = lax.axis_index("tensor")
    site_count = lax.axis_size("site")
    chunk = row_count // tensor_count
    row_start = tensor_index * chunk
    back_lag = 2 * (section_count - 1)
    tick_count = micro_count + back_lag
    last_fwd_tick = micro_count + section_count - 3
    first_bwd_tick = section_count - 1

    def my_rows(rows):
        return lax.dynamic_slice_in_dim(rows, row_start, chunk, axis=0)

    def hidden_of(normed):
        gate_pre = jnp.dot(normed, w_gate, preferred_element_type=jnp.float32)
        up_pre = jnp.dot(normed, w_up, preferred_element_type=jnp.float32)
        return (gate_pre, up_pre, jax.nn.sigmoid(gate_pre))

    def slot_of(micro_index):
        is_valid = (micro_index >= 0) & (micro_index < micro_count)
        return (is_valid, jnp.clip(micro_index, 0, micro_count - 1))

    weight_grads = (
        jnp.zeros(w_gate.shape, jnp.float32),
        jnp.zeros(w_up.shape, jnp.float32),
        jnp.zeros(w_down.shape, jnp.float32),
    )
    gain_grad = jnp.zeros((feature_count,), jnp.float32)
    stored = jnp.zeros((micro_count, row_count, feature_count), jnp.bfloat16)
    recv_fwd = jnp.zeros((chunk, feature_count), jnp.bfloat16)
    recv_bwd = jnp.zeros((chunk, feature_count), jnp.bfloat16)
    for moment in range(tick_count):
        do_fwd = moment <= last_fwd_tick + 1
        do_bwd = moment >= first_bwd_tick
        fwd_valid, fwd_slot = slot_of(moment - section_index)
        bwd_valid, bwd_slot = slot_of(moment - back_lag + section_index)
        pieces = []
        if do_fwd:
            if moment < micro_count:
                fwd_chunk = jnp.where(section_index == 0, my_rows(site_feed[moment]), recv_fwd)
            else:
                fwd_chunk = recv_fwd
            pieces.append(fwd_chunk)
        if do_bwd:
            own_grad = my_rows(pick_block(loss_grad, bwd_slot))
            bwd_chunk = jnp.where(section_index == section_count - 1, own_grad, recv_bwd)
            bwd_chunk = jnp.where(bwd_valid, bwd_chunk, jnp.zeros_like(bwd_chunk))
            pieces.append(bwd_chunk)
        if moment == 0:
            gathered = [site_feed[0]]
        else:
            gathered_all = gather_rows(jnp.stack(pieces), tensor_count)
            gathered = [gathered_all[i] for i in range(len(pieces))]
        parts = []
        if do_fwd:
            fwd_rows = gathered[0]
            previous = pick_block(stored, fwd_slot)
            stored = lax.dynamic_update_index_in_dim(
                stored, jnp.where(fwd_valid, fwd_rows, previous), fwd_slot, 0
            )
        if do_fwd and moment <= last_fwd_tick:
            wide_in = fwd_rows.astype(jnp.float32)
            unit_rows, row_scale, normed = norm_rows(wide_in, gain_row)
            make_gate_pre, make_up_pre, make_sig_gate = hidden_of(normed)
            partial_value = jnp.dot(
                (make_gate_pre * make_sig_gate * make_up_pre).astype(jnp.bfloat16),
                w_down,
                preferred_element_type=jnp.float32,
            )
            parts.append(partial_value.astype(jnp.bfloat16))
        if do_bwd:
            incoming = gathered[-1]
            wide_in = pick_block(stored, bwd_slot).astype(jnp.float32)
            unit_rows, row_scale, normed = norm_rows(wide_in, gain_row)
            local_gate_pre, local_up_pre, sig_gate = hidden_of(normed)
            silu_gate = local_gate_pre * sig_gate
            hidden = (silu_gate * local_up_pre).astype(jnp.bfloat16)
            d_hidden = contract_cols(incoming, w_down)
            d_gate_pre = (
                d_hidden * local_up_pre * sig_gate * (1.0 + local_gate_pre * (1.0 - sig_gate))
            ).astype(jnp.bfloat16)
            d_up_pre = (d_hidden * silu_gate).astype(jnp.bfloat16)
            weight_grads = (
                weight_grads[0] + contract_rows(normed, d_gate_pre),
                weight_grads[1] + contract_rows(normed, d_up_pre),
                weight_grads[2] + contract_rows(hidden, incoming),
            )
            d_part = contract_cols(d_gate_pre, w_gate) + contract_cols(d_up_pre, w_up)
            parts.append(d_part.astype(jnp.bfloat16))
        if not parts:
            continue
        reduced = scatter_rows(jnp.stack(parts), tensor_count)
        if do_fwd and moment <= last_fwd_tick:
            out_chunk = (fwd_chunk.astype(jnp.float32) + reduced[0]).astype(jnp.bfloat16)
            recv_fwd = passed_along(out_chunk, "section", 1)
        if do_bwd:
            d_norm = reduced[-1]
            unit_mine = my_rows(unit_rows)
            scale_mine = my_rows(row_scale)
            gain_grad = gain_grad + jnp.sum(d_norm * unit_mine, axis=0)
            if moment + 1 < tick_count:
                d_unit = d_norm * gain_row
                sent_back = (
                    bwd_chunk.astype(jnp.float32)
                    + scale_mine
                    * (d_unit - unit_mine * jnp.mean(d_unit * unit_mine, axis=-1, keepdims=True))
                ).astype(jnp.bfloat16)
                recv_bwd = passed_along(sent_back, "section", -1)
    gain_term = gain_grad + jnp.where(
        tensor_index == 0, prox_weight * (gain_row - anchor_gain[0]), jnp.zeros_like(gain_row)
    )
    gate_term = weight_grads[0] + prox_weight * (
        w_gate.astype(jnp.float32) - anchor_gate[0].astype(jnp.float32)
    )
    up_term = weight_grads[1] + prox_weight * (
        w_up.astype(jnp.float32) - anchor_up[0].astype(jnp.float32)
    )
    down_term = weight_grads[2] + prox_weight * (
        w_down.astype(jnp.float32) - anchor_down[0].astype(jnp.float32)
    )
    gate_total, up_total, down_total = (
        lax.psum(gate_term.astype(jnp.bfloat16), "site").astype(jnp.float32),
        lax.psum(up_term.astype(jnp.bfloat16), "site").astype(jnp.float32),
        lax.psum(down_term.astype(jnp.bfloat16), "site").astype(jnp.float32),
    )
    gain_total = lax.psum(gain_term, ("site", "tensor"))
    return (
        (gate_total / site_count)[None],
        (up_total / site_count)[None],
        (down_total / site_count)[None],
        (gain_total / site_count)[None],
    )


def solution(mesh):
    in_specs = (
        P("site", None, None, None),
        P("site", None, None, None),
        P("site", "section", None, "tensor"),
        P("site", "section", None, "tensor"),
        P("site", "section", "tensor", None),
        P("site", "section", None),
        P("section", None, "tensor"),
        P("section", None, "tensor"),
        P("section", "tensor", None),
        P("section", None),
    )
    out_specs = (
        P("section", None, "tensor"),
        P("section", None, "tensor"),
        P("section", "tensor", None),
        P("section", None),
    )
    return jax.shard_map(shards, mesh=mesh, in_specs=in_specs, out_specs=out_specs, check_vma=False)
```

time: 1440 us -> 606 us (0.42)
  waiting for transfers between devices: 1190 us -> 102 us
  blocking collectives: 5.78 us -> 117 us
  starting transfers between devices: 35.4 us -> 146 us
  local copies, waits for them, and re-layouts: 13.1 us -> 30.9 us
    psum x13 -> x0, waiting for transfers between devices: 1040 us -> none  [the longest x7 541 us: shards(): d_norm = lax.psum(d_part.astype(jnp.bfloat16), 'tensor').astype(jnp.float32)]
    all_to_all x0 -> x16, starting transfers between devices: none -> 113 us  [the longest x9 68.5 us: scatter_rows(): got = lax.all_to_all(split, 'tensor', 1, 1, tiled=False)]
    all_to_all x0 -> x16, waiting for transfers between devices: none -> 84.5 us  [the longest x9 56.2 us: scatter_rows(): got = lax.all_to_all(split, 'tensor', 1, 1, tiled=False)]
    psum x1, blocking collectives: 5.78 us -> 79 us  [shards(): gain_total = lax.psum(gain_term, ('site', 'tensor'))]
    psum x1, waiting for transfers between devices: 70.6 us -> 0.01 us  [shards(): lax.psum(gate_term.astype(jnp.bfloat16), 'site').astype(jnp.float32)]
    ppermute x12, waiting for transfers between devices: 72.3 us -> 17.5 us  [passed_along(): return lax.ppermute(block, axis, route)]
    all_to_all x0 -> x3, blocking collectives: none -> 38 us  [the longest x2 24.8 us: gather_rows(): got = lax.all_to_all(spread, 'tensor', 1, 1, tiled=False)]
  transfers between devices with their start and end apart: 26 -> 29, of which waited for: 26 -> 27; matrix products, arithmetic and copies ran while one was open for 4% -> 11% of each run, Pallas kernels for 0% -> 0%
where the time goes in v1:
time: 606 us; the launch traced here: 599 us
  starting transfers between devices  146 us (24%)
  matrix products  133 us (22%)
  blocking collectives  117 us (19%)
  waiting for transfers between devices  102 us (17%)
  other arithmetic  54.3 us (9%)
  local copies, waits for them, and re-layouts  30.9 us (5%)
  between operations  15.4 us (3%)
    psum x1, blocking collectives, shards(): gain_total = lax.psum(gain_term, ('site', 'tensor'))  79 us
    all_to_all x9, starting transfers between devices, scatter_rows(): got = lax.all_to_all(split, 'tensor', 1, 1, tiled=False)  68.5 us
    all_to_all x9, waiting for transfers between devices, scatter_rows(): got = lax.all_to_all(split, 'tensor', 1, 1, tiled=False)  56.2 us
    dot_general x21, matrix products, contract_rows(): lax.dot_general(left_side, right_side, (((0,), (0,)), ((), ())), preferre...  53.4 us
    all_to_all x7, starting transfers between devices, gather_rows(): got = lax.all_to_all(spread, 'tensor', 1, 1, tiled=False)  45 us
    ppermute x12, starting transfers between devices, passed_along(): return lax.ppermute(block, axis, route)  32.7 us
    all_to_all x7, waiting for transfers between devices, gather_rows(): got = lax.all_to_all(spread, 'tensor', 1, 1, tiled=False)  28.2 us
    dot_general x21, matrix products, contract_cols(): lax.dot_general(left_side, right_side, (((1,), (1,)), ((), ())), preferre...  26 us
  transfers between devices with their start and end apart: 29, of which 27 were waited for; matrix products, arithmetic and copies ran while one was open for 11% of the time, Pallas kernels for 0%

profile of v1, /device:TPU:28, one launch (start us, length us, event | category | flops | bytes accessed | tf_op | source)
XLA Modules:
  0.0 598.8 jit_solution(13709308356881927581)
XLA Ops:
  11.3 3.5 convolution_convert_fusion.5
  14.8 8.3 %all-to-all-start = ((bf16[1,8,32,896]{3,2,0,1:T(8,128)(2,1)}), bf16[1,8,32,896]{3,2,0,1:T(8,128)(2,1)S(1)}, u32[]{:S(2)}, u32[]{:S(2)}) async-start(bf16[1,8,32,896]{3,2,0,1:T(8,128)(2,1)} %bitcast.8), calls=%async_computation | async-start | bytes 917504 | tf_op jit(solution)/shard_map/all_to_all | solution.py:48
  23.0 2.5 fusion.324
  25.6 5.4 all-to-all-done
  31.1 3.1 collective-permute-start
  34.2 3.0 collective-permute-done
  38.0 12.4 %all_to_all.95 = bf16[1,8,32,896]{3,2,0,1:T(8,128)(2,1)S(1)} all-to-all(bf16[1,8,32,896]{3,2,0,1:T(8,128)(2,1)S(1)} %broadcast_in_dim.39), channel_id=1, replica_groups=mesh['site'=4,'section'=4,'tensor'=8] {'tensor'}, dimensions={1} | all-to-all | bytes 917504 | tf_op jit(solution)/shard_map/all_to_all | solution.py:41
  52.1 3.8 convolution_convert_fusion.4
  56.0 13.2 %all_to_all.96 = bf16[1,8,32,896]{3,2,0,1:T(8,128)(2,1)S(1)} all-to-all(bf16[1,8,32,896]{3,2,0,1:T(8,128)(2,1)} %bitcast.540), channel_id=1, replica_groups=mesh['site'=4,'section'=4,'tensor'=8] {'tensor'}, dimensions={1} | all-to-all | bytes 917504 | tf_op jit(solution)/shard_map/all_to_all | solution.py:48
  69.3 3.1 collective-permute-start.1
  72.4 2.9 collective-permute-done.1
  76.2 12.4 %all_to_all.97 = bf16[1,8,32,896]{3,2,0,1:T(8,128)(2,1)S(1)} all-to-all(bf16[1,8,32,896]{3,2,0,1:T(8,128)(2,1)S(1)} %broadcast_in_dim.40), channel_id=1, replica_groups=mesh['site'=4,'section'=4,'tensor'=8] {'tensor'}, dimensions={1} | all-to-all | bytes 917504 | tf_op jit(solution)/shard_map/all_to_all | solution.py:41
  91.1 4.0 convolution_convert_fusion.3
  95.1 6.3 %all-to-all-start.4 = ((bf16[1,8,32,896]{3,2,0,1:T(8,128)(2,1)}), bf16[1,8,32,896]{3,2,0,1:T(8,128)(2,1)S(1)}, u32[]{:S(2)}, u32[]{:S(2)}) async-start(bf16[1,8,32,896]{3,2,0,1:T(8,128)(2,1)} %bitcast.539), calls=%async_computation.4 | async-start | bytes 917504 | tf_op jit(solution)/shard_map/all_to_all | solution.py:48
  101.4 6.9 %all-to-all-done.4 = bf16[1,8,32,896]{3,2,0,1:T(8,128)(2,1)S(1)} async-done(((bf16[1,8,32,896]{3,2,0,1:T(8,128)(2,1)}), bf16[1,8,32,896]{3,2,0,1:T(8,128)(2,1)S(1)}, u32[]{:S(2)}, u32[]{:S(2)}) %all-to-all-start.4) | async-done | bytes 458784 | tf_op jit(solution)/shard_map/all_to_all | solution.py:48
  108.4 3.1 collective-permute-start.2
  116.3 6.8 %all-to-all-start.5 = ((bf16[2,8,32,896]{3,2,0,1:T(8,128)(2,1)}), bf16[2,8,32,896]{3,2,0,1:T(8,128)(2,1)}, u32[]{:S(2)}, u32[]{:S(2)}) async-start(bf16[2,8,32,896]{3,2,0,1:T(8,128)(2,1)} %broadcast_in_dim.41), calls=%async_computation.5 | async-start | bytes 1835008 | tf_op jit(solution)/shard_map/all_to_all | solution.py:41
  124.7 7.8 %all-to-all-done.5 = bf16[2,8,32,896]{3,2,0,1:T(8,128)(2,1)} async-done(((bf16[2,8,32,896]{3,2,0,1:T(8,128)(2,1)}), bf16[2,8,32,896]{3,2,0,1:T(8,128)(2,1)}, u32[]{:S(2)}, u32[]{:S(2)}) %all-to-all-start.5) | async-done | bytes 917536 | tf_op jit(solution)/shard_map/all_to_all | solution.py:41
  141.7 4.2 convolution_convert_fusion.2
  151.1 16.8 %all-to-all-start.6 = ((bf16[2,8,32,896]{3,2,0,1:T(8,128)(2,1)}), bf16[2,8,32,896]{3,2,0,1:T(8,128)(2,1)}, u32[]{:S(2)}, u32[]{:S(2)}) async-start(bf16[2,8,32,896]{3,2,0,1:T(8,128)(2,1)} %pad_maximum_fusion), calls=%async_computation.6 | async-start | bytes 1835008 | tf_op jit(solution)/shard_map/all_to_all | solution.py:48
  169.0 8.3 %all-to-all-done.6 = bf16[2,8,32,896]{3,2,0,1:T(8,128)(2,1)} async-done(((bf16[2,8,32,896]{3,2,0,1:T(8,128)(2,1)}), bf16[2,8,32,896]{3,2,0,1:T(8,128)(2,1)}, u32[]{:S(2)}, u32[]{:S(2)}) %all-to-all-start.6) | async-done | bytes 917536 | tf_op jit(solution)/shard_map/all_to_all | solution.py:48
  180.8 2.4 collective-permute-start.4
  183.3 3.4 collective-permute-start.3
  190.4 6.4 %all-to-all-start.7 = ((bf16[2,8,32,896]{3,2,0,1:T(8,128)(2,1)}), bf16[2,8,32,896]{3,2,0,1:T(8,128)(2,1)}, u32[]{:S(2)}, u32[]{:S(2)}) async-start(bf16[2,8,32,896]{3,2,0,1:T(8,128)(2,1)} %broadcast_in_dim.42), calls=%async_computation.7 | async-start | bytes 1835008 | tf_op jit(solution)/shard_map/all_to_all | solution.py:41
  198.7 2.9 fusion.223
  201.7 4.6 all-to-all-done.7
  215.4 4.2 convolution_convert_fusion.1
  224.8 6.4 %all-to-all-start.8 = ((bf16[2,8,32,896]{3,2,0,1:T(8,128)(2,1)}), bf16[2,8,32,896]{3,2,0,1:T(8,128)(2,1)}, u32[]{:S(2)}, u32[]{:S(2)}) async-start(bf16[2,8,32,896]{3,2,0,1:T(8,128)(2,1)} %pad_maximum_fusion.1), calls=%async_computation.8 | async-start | bytes 1835008 | tf_op jit(solution)/shard_map/all_to_all | solution.py:48
  232.3 8.3 %all-to-all-done.8 = bf16[2,8,32,896]{3,2,0,1:T(8,128)(2,1)} async-done(((bf16[2,8,32,896]{3,2,0,1:T(8,128)(2,1)}), bf16[2,8,32,896]{3,2,0,1:T(8,128)(2,1)}, u32[]{:S(2)}, u32[]{:S(2)}) %all-to-all-start.8) | async-done | bytes 917536 | tf_op jit(solution)/shard_map/all_to_all | solution.py:48
  246.1 3.9 collective-permute-start.5
  253.2 6.4 %all-to-all-start.9 = ((bf16[2,8,32,896]{3,2,0,1:T(8,128)(2,1)}), bf16[2,8,32,896]{3,2,0,1:T(8,128)(2,1)}, u32[]{:S(2)}, u32[]{:S(2)}) async-start(bf16[2,8,32,896]{3,2,0,1:T(8,128)(2,1)} %broadcast_in_dim.43), calls=%async_computation.9 | async-start | bytes 1835008 | tf_op jit(solution)/shard_map/all_to_all | solution.py:41
  261.5 3.0 fusion.225
  264.5 4.5 all-to-all-done.9
  278.1 4.2 convolution_convert_fusion
  287.7 6.4 %all-to-all-start.10 = ((bf16[2,8,32,896]{3,2,0,1:T(8,128)(2,1)}), bf16[2,8,32,896]{3,2,0,1:T(8,128)(2,1)}, u32[]{:S(2)}, u32[]{:S(2)}) async-start(bf16[2,8,32,896]{3,2,0,1:T(8,128)(2,1)} %pad_maximum_fusion.2), calls=%async_computation.10 | async-start | bytes 1835008 | tf_op jit(solution)/shard_map/all_to_all | solution.py:48
  294.1 3.1 fusion.210
  298.3 5.2 all-to-all-done.10
  311.0 4.0 collective-permute-start.7
  318.2 6.8 %all-to-all-start.11 = ((bf16[2,8,32,896]{3,2,0,1:T(8,128)(2,1)}), bf16[2,8,32,896]{3,2,0,1:T(8,128)(2,1)}, u32[]{:S(2)}, u32[]{:S(2)}) async-start(bf16[2,8,32,896]{3,2,0,1:T(8,128)(2,1)} %broadcast_in_dim.44), calls=%async_computation.11 | async-start | bytes 1835008 | tf_op jit(solution)/shard_map/all_to_all | solution.py:41
  330.9 3.6 all-to-all-done.11
  344.4 6.3 %all-to-all-start.12 = ((bf16[1,8,32,896]{3,2,0,1:T(8,128)(2,1)}), bf16[1,8,32,896]{3,2,0,1:T(8,128)(2,1)S(1)}, u32[]{:S(2)}, u32[]{:S(2)}) async-start(bf16[1,8,32,896]{3,2,0,1:T(8,128)(2,1)} %bitcast.530), calls=%async_computation.12 | async-start | bytes 917504 | tf_op jit(solution)/shard_map/all_to_all | solution.py:48
  352.9 7.0 %all-to-all-done.12 = bf16[1,8,32,896]{3,2,0,1:T(8,128)(2,1)S(1)} async-done(((bf16[1,8,32,896]{3,2,0,1:T(8,128)(2,1)}), bf16[1,8,32,896]{3,2,0,1:T(8,128)(2,1)S(1)}, u32[]{:S(2)}, u32[]{:S(2)}) %all-to-all-start.12) | async-done | bytes 458784 | tf_op jit(solution)/shard_map/all_to_all | solution.py:48
  365.5 2.7 collective-permute-done.9
  370.0 5.6 all-to-all-start.13
  375.6 2.7 fusion.57
  382.5 2.4 multiply_convert_fusion.18
  387.7 6.0 %all-to-all-start.14 = ((bf16[1,8,32,896]{3,2,0,1:T(8,128)(2,1)}), bf16[1,8,32,896]{3,2,0,1:T(8,128)(2,1)S(1)}, u32[]{:S(2)}, u32[]{:S(2)}) async-start(bf16[1,8,32,896]{3,2,0,1:T(8,128)(2,1)} %bitcast.532), calls=%async_computation.14 | async-start | bytes 917504 | tf_op jit(solution)/shard_map/all_to_all | solution.py:48
  397.3 3.4 all-to-all-done.14
  404.7 2.7 fusion.54
  410.6 6.2 %all-to-all-start.15 = ((bf16[1,8,32,896]{3,2,0,1:T(8,128)(2,1)}), bf16[1,8,32,896]{3,2,0,1:T(8,128)(2,1)S(1)}, u32[]{:S(2)}, u32[]{:S(2)}) async-start(bf16[1,8,32,896]{3,2,0,1:T(8,128)(2,1)} %broadcast_in_dim.46), calls=%async_computation.15 | async-start | bytes 917504 | tf_op jit(solution)/shard_map/all_to_all | solution.py:41
  420.3 3.4 all-to-all-done.15
  428.9 6.0 %all-to-all-start.16 = ((bf16[1,8,32,896]{3,2,0,1:T(8,128)(2,1)}), bf16[1,8,32,896]{3,2,0,1:T(8,128)(2,1)S(1)}, u32[]{:S(2)}, u32[]{:S(2)}) async-start(bf16[1,8,32,896]{3,2,0,1:T(8,128)(2,1)} %bitcast.531), calls=%async_computation.16 | async-start | bytes 917504 | tf_op jit(solution)/shard_map/all_to_all | solution.py:48
  435.0 3.0 fusion.230
  445.9 2.9 fusion.233
  451.8 6.8 %all-to-all-start.17 = ((bf16[1,8,32,896]{3,2,0,1:T(8,128)(2,1)}), bf16[1,8,32,896]{3,2,0,1:T(8,128)(2,1)}, u32[]{:S(2)}, u32[]{:S(2)}) async-start(bf16[1,8,32,896]{3,2,0,1:T(8,128)(2,1)} %broadcast_in_dim.47), calls=%async_computation.17 | async-start | bytes 917504 | tf_op jit(solution)/shard_map/all_to_all | solution.py:41
  458.6 3.0 fusion.232
  465.6 2.5 multiply_convert_fusion.14
  469.1 6.3 %fusion.3 = bf16[896,608]{0,1:T(8,128)(2,1)} fusion(f32[896,608]{0,1:T(8,128)} %fusion.233, f32[896,608]{0,1:T(8,128)} %fusion.231, f32[896,608]{0,1:T(8,128)} %fusion.229, f32[896,608]{0,1:T(8,128)} %fusion.227, f32[896,608]{0,1:T(8,128)S(1)} %copy-done.14, f32[896,608]{0,1:T(8,128)S(1)} %copy-done.16, bf16[256,608]{0,1:T(8,128)(2,1)S(1)} %get-tuple-element.31, ...), kind=kOutput, calls=%fused_computation.5 | convolution fusion | flops 285831168 | bytes 17118212 | tf_op jit(solution)/shard_map/dot_general | solution.py:23
  477.4 2.4 fusion.5
  483.4 3.4 fusion.1
  489.4 6.0 %all-to-all-start.18 = ((bf16[1,8,32,896]{3,2,0,1:T(8,128)(2,1)}), bf16[1,8,32,896]{3,2,0,1:T(8,128)(2,1)S(1)}, u32[]{:S(2)}, u32[]{:S(2)}) async-start(bf16[1,8,32,896]{3,2,0,1:T(8,128)(2,1)} %bitcast.93), calls=%async_computation.18 | async-start | bytes 917504 | tf_op jit(solution)/shard_map/all_to_all | solution.py:48
  495.5 9.7 %all-to-all-done.18 = bf16[1,8,32,896]{3,2,0,1:T(8,128)(2,1)S(1)} async-done(((bf16[1,8,32,896]{3,2,0,1:T(8,128)(2,1)}), bf16[1,8,32,896]{3,2,0,1:T(8,128)(2,1)S(1)}, u32[]{:S(2)}, u32[]{:S(2)}) %all-to-all-start.18) | async-done | bytes 458784 | tf_op jit(solution)/shard_map/all_to_all | solution.py:48
  506.2 79.0 %psum.31 = f32[896]{0:T(1024)S(1)} all-reduce(f32[896]{0:T(1024)S(1)} %select_add_fusion), channel_id=1, replica_groups=mesh['site'=4,'section'=4,'tensor'=8] {'site','tensor'}, use_global_device_ids=true, to_apply=%region_39.40 | all-reduce | flops 896 | bytes 7168 | tf_op jit(solution)/shard_map/psum | solution.py:200
  585.8 2.8 multiply_bitcast_fusion
  (340 shorter events, 173.4 us)
Async XLA Ops:
  7.2 4.1 copy-start.1
  7.2 4.1 copy-start.55
  14.8 16.2 %all-to-all-start = ((bf16[1,8,32,896]{3,2,0,1:T(8,128)(2,1)}), bf16[1,8,32,896]{3,2,0,1:T(8,128)(2,1)S(1)}, u32[]{:S(2)}, u32[]{:S(2)}) async-start(bf16[1,8,32,896]{3,2,0,1:T(8,128)(2,1)} %bitcast.8), calls=%async_computation | async-start | bytes 917504 | tf_op jit(solution)/shard_map/all_to_all | solution.py:48
  25.6 25.2 %copy-start = (bf16[1,1,896,608]{2,3,1,0:T(8,128)(2,1)S(1)}, bf16[1,1,896,608]{2,3,1,0:T(8,128)(2,1)}, u32[]{:S(2)}) copy-start(bf16[1,1,896,608]{2,3,1,0:T(8,128)(2,1)} %param.12) | copy-start | bytes 3268612
  31.1 6.1 %collective-permute-start = (bf16[32,896]{1,0:T(8,128)(2,1)S(1)}, bf16[32,896]{1,0:T(8,128)(2,1)S(1)}, u32[]{:S(2)}, u32[]{:S(2)}) collective-permute-start(bf16[32,896]{1,0:T(8,128)(2,1)S(1)} %fusion.244), channel_id=1, source_target_pairs={{0,8},{8,16},{16,24},{1,9},{9,17},{17,25},{2,10},{10,18},{18,26},{... | collective-permute-start | bytes 172040 | tf_op jit(solution)/shard_map/ppermute | solution.py:13
  69.3 6.1 %collective-permute-start.1 = (bf16[32,896]{1,0:T(8,128)(2,1)S(1)}, bf16[32,896]{1,0:T(8,128)(2,1)S(1)}, u32[]{:S(2)}, u32[]{:S(2)}) collective-permute-start(bf16[32,896]{1,0:T(8,128)(2,1)S(1)} %add_convert_fusion.6), channel_id=1, source_target_pairs={{0,8},{8,16},{16,24},{1,9},{9,17},{17,25},{2,10},{10,18},{18,26},{... | collective-permute-start | bytes 172040 | tf_op jit(solution)/shard_map/ppermute | solution.py:13
  88.6 6.5 %copy-start.27 = (bf16[1,8,32,896]{3,2,0,1:T(8,128)(2,1)}, bf16[1,8,32,896]{3,2,0,1:T(8,128)(2,1)S(1)}, u32[]{:S(2)}) copy-start(bf16[1,8,32,896]{3,2,0,1:T(8,128)(2,1)S(1)} %all_to_all.97) | copy-start | bytes 1376260
  95.1 13.2 %all-to-all-start.4 = ((bf16[1,8,32,896]{3,2,0,1:T(8,128)(2,1)}), bf16[1,8,32,896]{3,2,0,1:T(8,128)(2,1)S(1)}, u32[]{:S(2)}, u32[]{:S(2)}) async-start(bf16[1,8,32,896]{3,2,0,1:T(8,128)(2,1)} %bitcast.539), calls=%async_computation.4 | async-start | bytes 917504 | tf_op jit(solution)/shard_map/all_to_all | solution.py:48
  108.4 6.1 %collective-permute-start.2 = (bf16[32,896]{1,0:T(8,128)(2,1)S(1)}, bf16[32,896]{1,0:T(8,128)(2,1)S(1)}, u32[]{:S(2)}, u32[]{:S(2)}) collective-permute-start(bf16[32,896]{1,0:T(8,128)(2,1)S(1)} %add_convert_fusion.5), channel_id=1, source_target_pairs={{0,8},{8,16},{16,24},{1,9},{9,17},{17,25},{2,10},{10,18},{18,26},{... | collective-permute-start | bytes 172040 | tf_op jit(solution)/shard_map/ppermute | solution.py:13
  116.3 16.2 %all-to-all-start.5 = ((bf16[2,8,32,896]{3,2,0,1:T(8,128)(2,1)}), bf16[2,8,32,896]{3,2,0,1:T(8,128)(2,1)}, u32[]{:S(2)}, u32[]{:S(2)}) async-start(bf16[2,8,32,896]{3,2,0,1:T(8,128)(2,1)} %broadcast_in_dim.41), calls=%async_computation.5 | async-start | bytes 1835008 | tf_op jit(solution)/shard_map/all_to_all | solution.py:41
  151.1 26.2 %all-to-all-start.6 = ((bf16[2,8,32,896]{3,2,0,1:T(8,128)(2,1)}), bf16[2,8,32,896]{3,2,0,1:T(8,128)(2,1)}, u32[]{:S(2)}, u32[]{:S(2)}) async-start(bf16[2,8,32,896]{3,2,0,1:T(8,128)(2,1)} %pad_maximum_fusion), calls=%async_computation.6 | async-start | bytes 1835008 | tf_op jit(solution)/shard_map/all_to_all | solution.py:48
  180.8 6.1 %collective-permute-start.4 = (bf16[32,896]{1,0:T(8,128)(2,1)S(1)}, bf16[32,896]{1,0:T(8,128)(2,1)S(1)}, u32[]{:S(2)}, u32[]{:S(2)}) collective-permute-start(bf16[32,896]{1,0:T(8,128)(2,1)S(1)} %fusion.243), channel_id=1, source_target_pairs={{8,0},{16,8},{24,16},{9,1},{17,9},{25,17},{10,2},{18,10},{26,18},{... | collective-permute-start | bytes 172040 | tf_op jit(solution)/shard_map/ppermute | solution.py:13
  183.3 6.1 %collective-permute-start.3 = (bf16[32,896]{1,0:T(8,128)(2,1)S(1)}, bf16[32,896]{1,0:T(8,128)(2,1)S(1)}, u32[]{:S(2)}, u32[]{:S(2)}) collective-permute-start(bf16[32,896]{1,0:T(8,128)(2,1)S(1)} %get-tuple-element.55), channel_id=1, source_target_pairs={{0,8},{8,16},{16,24},{1,9},{9,17},{17,25},{2,10},{10,18},{18,26},{... | collective-permute-start | bytes 172040 | tf_op jit(solution)/shard_map/ppermute | solution.py:13
  190.4 15.8 %all-to-all-start.7 = ((bf16[2,8,32,896]{3,2,0,1:T(8,128)(2,1)}), bf16[2,8,32,896]{3,2,0,1:T(8,128)(2,1)}, u32[]{:S(2)}, u32[]{:S(2)}) async-start(bf16[2,8,32,896]{3,2,0,1:T(8,128)(2,1)} %broadcast_in_dim.42), calls=%async_computation.7 | async-start | bytes 1835008 | tf_op jit(solution)/shard_map/all_to_all | solution.py:41
  224.8 15.8 %all-to-all-start.8 = ((bf16[2,8,32,896]{3,2,0,1:T(8,128)(2,1)}), bf16[2,8,32,896]{3,2,0,1:T(8,128)(2,1)}, u32[]{:S(2)}, u32[]{:S(2)}) async-start(bf16[2,8,32,896]{3,2,0,1:T(8,128)(2,1)} %pad_maximum_fusion.1), calls=%async_computation.8 | async-start | bytes 1835008 | tf_op jit(solution)/shard_map/all_to_all | solution.py:48
  244.1 6.1 %collective-permute-start.6 = (bf16[32,896]{1,0:T(8,128)(2,1)S(1)}, bf16[32,896]{1,0:T(8,128)(2,1)S(1)}, u32[]{:S(2)}, u32[]{:S(2)}) collective-permute-start(bf16[32,896]{1,0:T(8,128)(2,1)S(1)} %add_convert_fusion.4), channel_id=1, source_target_pairs={{8,0},{16,8},{24,16},{9,1},{17,9},{25,17},{10,2},{18,10},{26,18},{... | collective-permute-start | bytes 172040 | tf_op jit(solution)/shard_map/ppermute | solution.py:13
  246.1 6.1 %collective-permute-start.5 = (bf16[32,896]{1,0:T(8,128)(2,1)S(1)}, bf16[32,896]{1,0:T(8,128)(2,1)S(1)}, u32[]{:S(2)}, u32[]{:S(2)}) collective-permute-start(bf16[32,896]{1,0:T(8,128)(2,1)S(1)} %get-tuple-element.54), channel_id=1, source_target_pairs={{0,8},{8,16},{16,24},{1,9},{9,17},{17,25},{2,10},{10,18},{18,26},{... | collective-permute-start | bytes 172040 | tf_op jit(solution)/shard_map/ppermute | solution.py:13
  253.2 15.8 %all-to-all-start.9 = ((bf16[2,8,32,896]{3,2,0,1:T(8,128)(2,1)}), bf16[2,8,32,896]{3,2,0,1:T(8,128)(2,1)}, u32[]{:S(2)}, u32[]{:S(2)}) async-start(bf16[2,8,32,896]{3,2,0,1:T(8,128)(2,1)} %broadcast_in_dim.43), calls=%async_computation.9 | async-start | bytes 1835008 | tf_op jit(solution)/shard_map/all_to_all | solution.py:41
  286.7 7.4 %copy-start.30 = (bf16[1,8,32,896]{3,2,0,1:T(8,128)(2,1)S(1)}, bf16[1,8,32,896]{3,2,0,1:T(8,128)(2,1)}, u32[]{:S(2)}) copy-start(bf16[1,8,32,896]{3,2,0,1:T(8,128)(2,1)} %get-tuple-element.51) | copy-start | bytes 1376260
  287.7 15.8 %all-to-all-start.10 = ((bf16[2,8,32,896]{3,2,0,1:T(8,128)(2,1)}), bf16[2,8,32,896]{3,2,0,1:T(8,128)(2,1)}, u32[]{:S(2)}, u32[]{:S(2)}) async-start(bf16[2,8,32,896]{3,2,0,1:T(8,128)(2,1)} %pad_maximum_fusion.2), calls=%async_computation.10 | async-start | bytes 1835008 | tf_op jit(solution)/shard_map/all_to_all | solution.py:48
  297.2 11.8 %copy-start.31 = (bf16[1,8,32,896]{3,2,0,1:T(8,128)(2,1)S(1)}, bf16[1,8,32,896]{3,2,0,1:T(8,128)(2,1)}, u32[]{:S(2)}) copy-start(bf16[1,8,32,896]{3,2,0,1:T(8,128)(2,1)} %get-tuple-element.49) | copy-start | bytes 1376260
  303.5 5.5 copy-start.63
  303.5 5.5 copy-start.64
  307.1 8.0 %collective-permute-start.8 = (bf16[32,896]{1,0:T(8,128)(2,1)S(1)}, bf16[32,896]{1,0:T(8,128)(2,1)S(1)}, u32[]{:S(2)}, u32[]{:S(2)}) collective-permute-start(bf16[32,896]{1,0:T(8,128)(2,1)S(1)} %add_convert_fusion.3), channel_id=1, source_target_pairs={{8,0},{16,8},{24,16},{9,1},{17,9},{25,17},{10,2},{18,10},{26,18},{... | collective-permute-start | bytes 172040 | tf_op jit(solution)/shard_map/ppermute | solution.py:13
  311.0 14.1 %copy-start.40 = (bf16[256,608]{0,1:T(8,128)(2,1)S(1)}, bf16[256,608]{0,1:T(8,128)(2,1)}, u32[]{:S(2)}) copy-start(bf16[256,608]{0,1:T(8,128)(2,1)} %copy-done.39) | copy-start | bytes 933892
  311.0 6.2 %collective-permute-start.7 = (bf16[32,896]{1,0:T(8,128)(2,1)S(1)}, bf16[32,896]{1,0:T(8,128)(2,1)S(1)}, u32[]{:S(2)}, u32[]{:S(2)}) collective-permute-start(bf16[32,896]{1,0:T(8,128)(2,1)S(1)} %get-tuple-element.53), channel_id=1, source_target_pairs={{0,8},{8,16},{16,24},{1,9},{9,17},{17,25},{2,10},{10,18},{18,26},{... | collective-permute-start | bytes 172040 | tf_op jit(solution)/shard_map/ppermute | solution.py:13
  318.2 16.3 %all-to-all-start.11 = ((bf16[2,8,32,896]{3,2,0,1:T(8,128)(2,1)}), bf16[2,8,32,896]{3,2,0,1:T(8,128)(2,1)}, u32[]{:S(2)}, u32[]{:S(2)}) async-start(bf16[2,8,32,896]{3,2,0,1:T(8,128)(2,1)} %broadcast_in_dim.44), calls=%async_computation.11 | async-start | bytes 1835008 | tf_op jit(solution)/shard_map/all_to_all | solution.py:41
  335.7 4.1 copy-start.33
  344.4 15.6 %all-to-all-start.12 = ((bf16[1,8,32,896]{3,2,0,1:T(8,128)(2,1)}), bf16[1,8,32,896]{3,2,0,1:T(8,128)(2,1)S(1)}, u32[]{:S(2)}, u32[]{:S(2)}) async-start(bf16[1,8,32,896]{3,2,0,1:T(8,128)(2,1)} %bitcast.530), calls=%async_computation.12 | async-start | bytes 917504 | tf_op jit(solution)/shard_map/all_to_all | solution.py:48
  362.2 6.1 %collective-permute-start.9 = (bf16[32,896]{1,0:T(8,128)(2,1)S(1)}, bf16[32,896]{1,0:T(8,128)(2,1)S(1)}, u32[]{:S(2)}, u32[]{:S(2)}) collective-permute-start(bf16[32,896]{1,0:T(8,128)(2,1)S(1)} %add_convert_fusion.2), channel_id=1, source_target_pairs={{8,0},{16,8},{24,16},{9,1},{17,9},{25,17},{10,2},{18,10},{26,18},{... | collective-permute-start | bytes 172040 | tf_op jit(solution)/shard_map/ppermute | solution.py:13
  370.0 12.5 %all-to-all-start.13 = ((bf16[1,8,32,896]{3,2,0,1:T(8,128)(2,1)}), bf16[1,8,32,896]{3,2,0,1:T(8,128)(2,1)S(1)}, u32[]{:S(2)}, u32[]{:S(2)}) async-start(bf16[1,8,32,896]{3,2,0,1:T(8,128)(2,1)} %broadcast_in_dim.45), calls=%async_computation.13 | async-start | bytes 917504 | tf_op jit(solution)/shard_map/all_to_all | solution.py:41
  384.9 2.9 copy-start.41
  387.7 12.9 %all-to-all-start.14 = ((bf16[1,8,32,896]{3,2,0,1:T(8,128)(2,1)}), bf16[1,8,32,896]{3,2,0,1:T(8,128)(2,1)S(1)}, u32[]{:S(2)}, u32[]{:S(2)}) async-start(bf16[1,8,32,896]{3,2,0,1:T(8,128)(2,1)} %bitcast.532), calls=%async_computation.14 | async-start | bytes 917504 | tf_op jit(solution)/shard_map/all_to_all | solution.py:48
  402.8 6.1 %collective-permute-start.10 = (bf16[32,896]{1,0:T(8,128)(2,1)S(1)}, bf16[32,896]{1,0:T(8,128)(2,1)S(1)}, u32[]{:S(2)}, u32[]{:S(2)}) collective-permute-start(bf16[32,896]{1,0:T(8,128)(2,1)S(1)} %add_convert_fusion.1), channel_id=1, source_target_pairs={{8,0},{16,8},{24,16},{9,1},{17,9},{25,17},{10,2},{18,10},{26,18},{... | collective-permute-start | bytes 172040 | tf_op jit(solution)/shard_map/ppermute | solution.py:13
  410.6 13.1 %all-to-all-start.15 = ((bf16[1,8,32,896]{3,2,0,1:T(8,128)(2,1)}), bf16[1,8,32,896]{3,2,0,1:T(8,128)(2,1)S(1)}, u32[]{:S(2)}, u32[]{:S(2)}) async-start(bf16[1,8,32,896]{3,2,0,1:T(8,128)(2,1)} %broadcast_in_dim.46), calls=%async_computation.15 | async-start | bytes 917504 | tf_op jit(solution)/shard_map/all_to_all | solution.py:41
  428.9 12.9 %all-to-all-start.16 = ((bf16[1,8,32,896]{3,2,0,1:T(8,128)(2,1)}), bf16[1,8,32,896]{3,2,0,1:T(8,128)(2,1)S(1)}, u32[]{:S(2)}, u32[]{:S(2)}) async-start(bf16[1,8,32,896]{3,2,0,1:T(8,128)(2,1)} %bitcast.531), calls=%async_computation.16 | async-start | bytes 917504 | tf_op jit(solution)/shard_map/all_to_all | solution.py:48
  434.9 3.1 copy-start.36
  434.9 3.1 copy-start.65
  435.0 3.1 copy-start.70
  444.0 6.1 %collective-permute-start.11 = (bf16[32,896]{1,0:T(8,128)(2,1)S(1)}, bf16[32,896]{1,0:T(8,128)(2,1)S(1)}, u32[]{:S(2)}, u32[]{:S(2)}) collective-permute-start(bf16[32,896]{1,0:T(8,128)(2,1)S(1)} %add_convert_fusion), channel_id=1, source_target_pairs={{8,0},{16,8},{24,16},{9,1},{17,9},{25,17},{10,2},{18,10},{26,18},{... | collective-permute-start | bytes 172040 | tf_op jit(solution)/shard_map/ppermute | solution.py:13
  451.8 9.8 %copy-start.38 = (bf16[1,8,32,896]{3,2,0,1:T(8,128)(2,1)S(1)}, bf16[1,8,32,896]{3,2,0,1:T(8,128)(2,1)}, u32[]{:S(2)}) copy-start(bf16[1,8,32,896]{3,2,0,1:T(8,128)(2,1)} %copy-done.37) | copy-start | bytes 1376260
  451.8 13.8 %all-to-all-start.17 = ((bf16[1,8,32,896]{3,2,0,1:T(8,128)(2,1)}), bf16[1,8,32,896]{3,2,0,1:T(8,128)(2,1)}, u32[]{:S(2)}, u32[]{:S(2)}) async-start(bf16[1,8,32,896]{3,2,0,1:T(8,128)(2,1)} %broadcast_in_dim.47), calls=%async_computation.17 | async-start | bytes 917504 | tf_op jit(solution)/shard_map/all_to_all | solution.py:41
  458.5 127.2 %all-reduce.3.cloned.1.call-start = ((), (), s32[]{:S(2)}) async-start(), calls=%async_computation.19 | async-start | bytes 6537216 | tf_op jit(solution)/shard_map/psum | solution.py:196
  458.6 3.0 copy-start.68
  458.6 3.0 copy-start.69
  465.6 3.4 copy-start.16
  468.0 7.4 %copy-start.52 = (bf16[256,608]{0,1:T(8,128)(2,1)}, bf16[256,608]{0,1:T(8,128)(2,1)S(1)}, u32[]{:S(2)}) copy-start(bf16[256,608]{0,1:T(8,128)(2,1)S(1)} %get-tuple-element.31) | copy-start | bytes 933892
  469.0 6.4 %copy-start.13 = (f32[896,608]{0,1:T(8,128)S(1)}, f32[896,608]{0,1:T(8,128)}, u32[]{:S(2)}) copy-start(f32[896,608]{0,1:T(8,128)} %fusion.222) | copy-start | bytes 6537220
  469.0 6.4 %copy-start.15 = (f32[896,608]{0,1:T(8,128)S(1)}, f32[896,608]{0,1:T(8,128)}, u32[]{:S(2)}) copy-start(f32[896,608]{0,1:T(8,128)} %fusion.224) | copy-start | bytes 6537220
  469.0 6.4 %copy-start.17 = (f32[896,608]{0,1:T(8,128)S(1)}, f32[896,608]{0,1:T(8,128)}, u32[]{:S(2)}) copy-start(f32[896,608]{0,1:T(8,128)} %fusion.226) | copy-start | bytes 6537220
  469.0 6.4 %copy-start.18 = (f32[896,608]{0,1:T(8,128)S(1)}, f32[896,608]{0,1:T(8,128)}, u32[]{:S(2)}) copy-start(f32[896,608]{0,1:T(8,128)} %fusion.228) | copy-start | bytes 6537220
  469.0 7.4 %copy-start.19 = (f32[896,608]{0,1:T(8,128)S(1)}, f32[896,608]{0,1:T(8,128)}, u32[]{:S(2)}) copy-start(f32[896,608]{0,1:T(8,128)} %fusion.230) | copy-start | bytes 6537220
  469.0 8.0 %copy-start.20 = (f32[896,608]{0,1:T(8,128)S(1)}, f32[896,608]{0,1:T(8,128)}, u32[]{:S(2)}) copy-start(f32[896,608]{0,1:T(8,128)} %fusion.232) | copy-start | bytes 6537220
  469.0 8.3 %copy-start.54 = (bf16[1,896,608]{1,2,0:T(8,128)(2,1)S(1)}, bf16[1,896,608]{1,2,0:T(8,128)(2,1)}, u32[]{:S(2)}) copy-start(bf16[1,896,608]{1,2,0:T(8,128)(2,1)} %param.16) | copy-start | bytes 3268612
  477.3 3.3 copy-start.23
  477.3 3.9 copy-start.24
  477.3 4.6 copy-start.25
  477.3 5.2 copy-start.26
  477.3 5.4 copy-start.57
  477.3 5.7 copy-start.58
  477.4 5.8 copy-start.61
  477.4 6.0 %copy-start.62 = (f32[256,608]{0,1:T(8,128)S(1)}, f32[256,608]{0,1:T(8,128)}, u32[]{:S(2)}) copy-start(f32[256,608]{0,1:T(8,128)} %fusion.88) | copy-start | bytes 1867780
  488.1 7.4 %copy-start.78 = (f32[1,896]{1,0:T(1,128)S(1)}, f32[1,896]{1,0:T(1,128)}, u32[]{:S(2)}) copy-start(f32[1,896]{1,0:T(1,128)} %param.19) | copy-start | bytes 10756
  489.4 15.8 %all-to-all-start.18 = ((bf16[1,8,32,896]{3,2,0,1:T(8,128)(2,1)}), bf16[1,8,32,896]{3,2,0,1:T(8,128)(2,1)S(1)}, u32[]{:S(2)}, u32[]{:S(2)}) async-start(bf16[1,8,32,896]{3,2,0,1:T(8,128)(2,1)} %bitcast.93), calls=%async_computation.18 | async-start | bytes 917504 | tf_op jit(solution)/shard_map/all_to_all | solution.py:48
  (44 other events, 85.0 us)
Sparse Core Ops, SparseCore 0:
  486.9 77.7 all-reduce.2
